TPU v7x, 32 devices: a whole 2x2x4 slice. The times are simulated.
32 devices in a mesh: grp: 2 (over y), row: 4 (over z), col: 2 (over x), vec: 2 (over core).
Axes of the slice: x: 2, y: 2, z: 4, core: 2. Of those that a mesh axis runs over, the one named last changes fastest.
Arguments:
- start: float32 [64, 2048], P('vec', ('grp', 'row')), parts along dimension 1, may hold values from -6 to 6
- tiles: bfloat16 [16, 32, 128, 128], P(('grp', 'row'), 'col'), parts along dimension 0, may hold values from -6 to 6
- pattern: int32 [16, 32], P(('grp', 'row')), parts along dimension 0, may hold values from 0 to 7
- counts: int32 [16], P(('grp', 'row')), parts along dimension 0, may hold values from 1 to 32
Outputs:
- basis: float32 [64, 2048], P('vec', ('grp', 'row')), parts along dimension 1
There are 2 independent parts, one for each index of `grp`. A program takes and returns all parts, laid end to end along the dimension named above; each array names one. Nothing has to cross between parts.
Inputs may be any that keep to these rules, and one draw needn't show every extreme that they name: pattern may name a block column more than once in a block row; such tiles add.
All inputs are finite; a program needn't handle non-finite values.
Results may differ from a plain program's by a relative error of at most 0.03.
Values may be sent and summed in bfloat16 or wider, within the bound.
No kernel may reach another device: no remote copies, remote signals or barrier semaphores. Data moves between devices by JAX's collectives and lax.ppermute only.
A program may use at most 64 MiB of HBM per device.

v0:
```python
import jax
import jax.numpy as jnp
from jax import lax
from jax.sharding import PartitionSpec as P

DEGREE = 8
ITERS = 2
HALF_WIDTH = 2.0
EPSILON = 1e-06


def row_scaling(square_sums, live_counts, block):
    entries = (live_counts * block).astype(jnp.float32)[:, None]
    scaled = lax.rsqrt(square_sums / entries + EPSILON) / jnp.sqrt(entries)
    return (scaled / HALF_WIDTH).reshape(1, -1)


def chebyshev(first, apply):
    previous = first
    present = apply(first)
    for step in range(DEGREE - 1):
        previous, present = (present, 2.0 * apply(present) - previous)
    return present


def orthonormal(mine, total_rows):
    both = lax.all_gather(mine.astype(jnp.bfloat16), "vec", axis=0, tiled=True).astype(mine.dtype)
    part_gram = jnp.dot(both, both.T, precision=lax.Precision.HIGHEST)
    gram = lax.psum(part_gram, "row") / total_rows
    lower = jnp.linalg.cholesky(gram)
    solved = jax.scipy.linalg.solve_triangular(lower, both, lower=True)
    width = mine.shape[0]
    return lax.dynamic_slice_in_dim(solved, lax.axis_index("vec") * width, width, 0)


def per_device(start, tiles, pattern, counts):
    nb_dev = tiles.shape[0]
    block = tiles.shape[2]
    total_rows = nb_dev * block * lax.axis_size("row")
    vec_cols = start.shape[0]
    col_index = lax.axis_index("col")
    kb_dev = tiles.shape[1]
    slot_ids = col_index * kb_dev + jnp.arange(kb_dev, dtype=jnp.int32)
    live = (slot_ids[None, :] < counts[:, None]).astype(jnp.bfloat16)
    masked = tiles * live[:, :, None, None]
    local_pattern = lax.dynamic_slice_in_dim(pattern, col_index * kb_dev, kb_dev, 1)
    partial_squares = jnp.einsum(
        "bkmn,bkmn->bm", masked, masked, preferred_element_type=jnp.float32
    )
    square_sums = lax.psum(partial_squares, "col")
    scaling = row_scaling(square_sums, counts, block)

    def apply_slots(current):
        whole = lax.all_gather(current.astype(jnp.bfloat16), "row", axis=1, tiled=True)
        blocks = whole.reshape(vec_cols, -1, block)
        picked = jnp.take(blocks, local_pattern, axis=1)
        product = jnp.einsum("cbkn,bkmn->cbm", picked, masked, preferred_element_type=jnp.float32)
        total = lax.psum(product.astype(jnp.bfloat16), "col").astype(jnp.float32)
        return total.reshape(vec_cols, -1) * scaling

    current = start
    for outer in range(ITERS):
        filtered = chebyshev(current, apply_slots)
        current = orthonormal(filtered, total_rows)
    return current


def solution(mesh):
    in_specs = (
        P("vec", ("grp", "row")),
        P(("grp", "row"), "col", None, None),
        P(("grp", "row"), None),
        P(("grp", "row")),
    )
    out_specs = P("vec", ("grp", "row"))
    return jax.shard_map(
        per_device, mesh=mesh, in_specs=in_specs, out_specs=out_specs, check_vma=False
    )
```

profile of v0, /device:TPU:0, one launch (start us, length us, event | category | flops | bytes accessed | tf_op | source)
XLA Modules:
  0.0 427.7 jit_solution(17464882422868183498)
XLA Ops:
  9.9 14.0 %all_gather.54 = bf16[32,1024]{1,0:T(8,128)(2,1)S(1)} all-gather(bf16[32,256]{1,0:T(8,128)(2,1)S(1)} %convert_element_type.183), channel_id=1, replica_groups=mesh['grp'=2,'row'=4,'col'=2,'vec'=2] {'row'}, dimensions={1}, use_global_device_ids=true | all-gather | bytes 81920 | tf_op jit(solution)/shard_map/all_gather | solution.py:54
  25.1 8.2 %psum.133 = bf16[32,256]{1,0:T(8,128)(2,1)S(1)} all-reduce(bf16[32,256]{1,0:T(8,128)(2,1)S(1)} %bitcast.395), channel_id=1, replica_groups=mesh['grp'=2,'row'=4,'col'=2,'vec'=2] {'col'}, use_global_device_ids=true, to_apply=%region_0.2 | all-reduce | flops 8192 | bytes 32768 | tf_op jit(solution)/shard_map/psum | solution.py:58
  33.3 13.2 %all_gather.55 = bf16[32,1024]{1,0:T(8,128)(2,1)S(1)} all-gather(bf16[32,256]{1,0:T(8,128)(2,1)S(1)} %fusion.110), channel_id=1, replica_groups=mesh['grp'=2,'row'=4,'col'=2,'vec'=2] {'row'}, dimensions={1}, use_global_device_ids=true | all-gather | bytes 81920 | tf_op jit(solution)/shard_map/all_gather | solution.py:54
  54.8 13.3 %all_gather.56 = bf16[32,1024]{1,0:T(8,128)(2,1)S(1)} all-gather(bf16[32,256]{1,0:T(8,128)(2,1)S(1)} %fusion.113), channel_id=1, replica_groups=mesh['grp'=2,'row'=4,'col'=2,'vec'=2] {'row'}, dimensions={1}, use_global_device_ids=true | all-gather | bytes 81920 | tf_op jit(solution)/shard_map/all_gather | solution.py:54
  69.2 8.1 %psum.136 = bf16[32,256]{1,0:T(8,128)(2,1)S(1)} all-reduce(bf16[32,256]{1,0:T(8,128)(2,1)S(1)} %bitcast.397), channel_id=1, replica_groups=mesh['grp'=2,'row'=4,'col'=2,'vec'=2] {'col'}, use_global_device_ids=true, to_apply=%region_3.5 | all-reduce | flops 8192 | bytes 32768 | tf_op jit(solution)/shard_map/psum | solution.py:58
  77.4 13.2 %all_gather.57 = bf16[32,1024]{1,0:T(8,128)(2,1)S(1)} all-gather(bf16[32,256]{1,0:T(8,128)(2,1)S(1)} %fusion.111), channel_id=1, replica_groups=mesh['grp'=2,'row'=4,'col'=2,'vec'=2] {'row'}, dimensions={1}, use_global_device_ids=true | all-gather | bytes 81920 | tf_op jit(solution)/shard_map/all_gather | solution.py:54
  98.9 13.2 %all_gather.58 = bf16[32,1024]{1,0:T(8,128)(2,1)S(1)} all-gather(bf16[32,256]{1,0:T(8,128)(2,1)S(1)} %fusion.137), channel_id=1, replica_groups=mesh['grp'=2,'row'=4,'col'=2,'vec'=2] {'row'}, dimensions={1}, use_global_device_ids=true | all-gather | bytes 81920 | tf_op jit(solution)/shard_map/all_gather | solution.py:54
  113.3 8.1 %psum.138 = bf16[32,256]{1,0:T(8,128)(2,1)S(1)} all-reduce(bf16[32,256]{1,0:T(8,128)(2,1)S(1)} %bitcast.399), channel_id=1, replica_groups=mesh['grp'=2,'row'=4,'col'=2,'vec'=2] {'col'}, use_global_device_ids=true, to_apply=%region_5.7 | all-reduce | flops 8192 | bytes 32768 | tf_op jit(solution)/shard_map/psum | solution.py:58
  121.5 13.1 %all_gather.59 = bf16[32,1024]{1,0:T(8,128)(2,1)S(1)} all-gather(bf16[32,256]{1,0:T(8,128)(2,1)S(1)} %fusion.116), channel_id=1, replica_groups=mesh['grp'=2,'row'=4,'col'=2,'vec'=2] {'row'}, dimensions={1}, use_global_device_ids=true | all-gather | bytes 81920 | tf_op jit(solution)/shard_map/all_gather | solution.py:54
  143.1 13.2 %all_gather.60 = bf16[32,1024]{1,0:T(8,128)(2,1)S(1)} all-gather(bf16[32,256]{1,0:T(8,128)(2,1)S(1)} %fusion.114), channel_id=1, replica_groups=mesh['grp'=2,'row'=4,'col'=2,'vec'=2] {'row'}, dimensions={1}, use_global_device_ids=true | all-gather | bytes 81920 | tf_op jit(solution)/shard_map/all_gather | solution.py:54
  157.4 8.0 %psum.140 = bf16[32,256]{1,0:T(8,128)(2,1)S(1)} all-reduce(bf16[32,256]{1,0:T(8,128)(2,1)S(1)} %bitcast.401), channel_id=1, replica_groups=mesh['grp'=2,'row'=4,'col'=2,'vec'=2] {'col'}, use_global_device_ids=true, to_apply=%region_7.9 | all-reduce | flops 8192 | bytes 32768 | tf_op jit(solution)/shard_map/psum | solution.py:58
  165.5 13.1 %all_gather.61 = bf16[32,1024]{1,0:T(8,128)(2,1)S(1)} all-gather(bf16[32,256]{1,0:T(8,128)(2,1)S(1)} %subtract_convert_fusion.3), channel_id=1, replica_groups=mesh['grp'=2,'row'=4,'col'=2,'vec'=2] {'row'}, dimensions={1}, use_global_device_ids=true | all-gather | bytes 81920 | tf_op jit(solution)/shard_map/all_gather | solution.py:54
  189.1 18.8 %psum.142 = f32[64,64]{0,1:T(8,128)S(1)} all-reduce(f32[64,64]{0,1:T(8,128)S(1)} %fusion.138), channel_id=1, replica_groups=mesh['grp'=2,'row'=4,'col'=2,'vec'=2] {'row'}, use_global_device_ids=true, to_apply=%region_9.11 | all-reduce | flops 4096 | bytes 32768 | tf_op jit(solution)/shard_map/psum | solution.py:29
  220.4 13.1 %all_gather.63 = bf16[32,1024]{1,0:T(8,128)(2,1)S(1)} all-gather(bf16[32,256]{1,0:T(8,128)(2,1)S(1)} %dynamic-slice_convert_fusion), channel_id=1, replica_groups=mesh['grp'=2,'row'=4,'col'=2,'vec'=2] {'row'}, dimensions={1}, use_global_device_ids=true | all-gather | bytes 81920 | tf_op jit(solution)/shard_map/all_gather | solution.py:54
  234.7 8.0 %psum.143 = bf16[32,256]{1,0:T(8,128)(2,1)S(1)} all-reduce(bf16[32,256]{1,0:T(8,128)(2,1)S(1)} %bitcast.403), channel_id=1, replica_groups=mesh['grp'=2,'row'=4,'col'=2,'vec'=2] {'col'}, use_global_device_ids=true, to_apply=%region_12.16 | all-reduce | flops 8192 | bytes 32768 | tf_op jit(solution)/shard_map/psum | solution.py:58
  242.8 13.2 %all_gather.64 = bf16[32,1024]{1,0:T(8,128)(2,1)S(1)} all-gather(bf16[32,256]{1,0:T(8,128)(2,1)S(1)} %fusion.109), channel_id=1, replica_groups=mesh['grp'=2,'row'=4,'col'=2,'vec'=2] {'row'}, dimensions={1}, use_global_device_ids=true | all-gather | bytes 81920 | tf_op jit(solution)/shard_map/all_gather | solution.py:54
  264.4 13.1 %all_gather.65 = bf16[32,1024]{1,0:T(8,128)(2,1)S(1)} all-gather(bf16[32,256]{1,0:T(8,128)(2,1)S(1)} %fusion.136), channel_id=1, replica_groups=mesh['grp'=2,'row'=4,'col'=2,'vec'=2] {'row'}, dimensions={1}, use_global_device_ids=true | all-gather | bytes 81920 | tf_op jit(solution)/shard_map/all_gather | solution.py:54
  278.8 8.0 %psum.145 = bf16[32,256]{1,0:T(8,128)(2,1)S(1)} all-reduce(bf16[32,256]{1,0:T(8,128)(2,1)S(1)} %bitcast.405), channel_id=1, replica_groups=mesh['grp'=2,'row'=4,'col'=2,'vec'=2] {'col'}, use_global_device_ids=true, to_apply=%region_14.18 | all-reduce | flops 8192 | bytes 32768 | tf_op jit(solution)/shard_map/psum | solution.py:58
  286.8 13.1 %all_gather.66 = bf16[32,1024]{1,0:T(8,128)(2,1)S(1)} all-gather(bf16[32,256]{1,0:T(8,128)(2,1)S(1)} %fusion.112), channel_id=1, replica_groups=mesh['grp'=2,'row'=4,'col'=2,'vec'=2] {'row'}, dimensions={1}, use_global_device_ids=true | all-gather | bytes 81920 | tf_op jit(solution)/shard_map/all_gather | solution.py:54
  308.5 13.2 %all_gather.67 = bf16[32,1024]{1,0:T(8,128)(2,1)S(1)} all-gather(bf16[32,256]{1,0:T(8,128)(2,1)S(1)} %fusion.115), channel_id=1, replica_groups=mesh['grp'=2,'row'=4,'col'=2,'vec'=2] {'row'}, dimensions={1}, use_global_device_ids=true | all-gather | bytes 81920 | tf_op jit(solution)/shard_map/all_gather | solution.py:54
  330.8 13.3 %all_gather.68 = bf16[32,1024]{1,0:T(8,128)(2,1)S(1)} all-gather(bf16[32,256]{1,0:T(8,128)(2,1)S(1)} %fusion.117), channel_id=1, replica_groups=mesh['grp'=2,'row'=4,'col'=2,'vec'=2] {'row'}, dimensions={1}, use_global_device_ids=true | all-gather | bytes 81920 | tf_op jit(solution)/shard_map/all_gather | solution.py:54
  352.7 13.1 %all_gather.69 = bf16[32,1024]{1,0:T(8,128)(2,1)S(1)} all-gather(bf16[32,256]{1,0:T(8,128)(2,1)S(1)} %fusion.118), channel_id=1, replica_groups=mesh['grp'=2,'row'=4,'col'=2,'vec'=2] {'row'}, dimensions={1}, use_global_device_ids=true | all-gather | bytes 81920 | tf_op jit(solution)/shard_map/all_gather | solution.py:54
  375.0 13.1 %all_gather.70 = bf16[32,1024]{1,0:T(8,128)(2,1)S(1)} all-gather(bf16[32,256]{1,0:T(8,128)(2,1)S(1)} %subtract_convert_fusion.1), channel_id=1, replica_groups=mesh['grp'=2,'row'=4,'col'=2,'vec'=2] {'row'}, dimensions={1}, use_global_device_ids=true | all-gather | bytes 81920 | tf_op jit(solution)/shard_map/all_gather | solution.py:54
  398.7 15.9 %psum.151 = f32[64,64]{0,1:T(8,128)S(1)} all-reduce(f32[64,64]{0,1:T(8,128)S(1)} %fusion.139), channel_id=1, replica_groups=mesh['grp'=2,'row'=4,'col'=2,'vec'=2] {'row'}, use_global_device_ids=true, to_apply=%region_20.24 | all-reduce | flops 4096 | bytes 32768 | tf_op jit(solution)/shard_map/psum | solution.py:29
  (131 shorter events, 132.3 us)
Async XLA Ops:
  0.0 24.5 %copy-start = (bf16[2,16,128,128]{3,2,1,0:T(8,128)(2,1)S(1)}, bf16[2,16,128,128]{3,2,1,0:T(8,128)(2,1)}, u32[]{:S(2)}) copy-start(bf16[2,16,128,128]{3,2,1,0:T(8,128)(2,1)} %param.10) | copy-start | bytes 3145732
  0.0 9.9 %copy-start.1 = (f32[32,256]{1,0:T(8,128)S(1)}, f32[32,256]{1,0:T(8,128)}, u32[]{:S(2)}) copy-start(f32[32,256]{1,0:T(8,128)} %param.9) | copy-start | bytes 98308
  0.0 9.7 %copy-start.2 = (s32[2,32]{1,0:T(2,128)S(1)}, s32[2,32]{1,0:T(2,128)}, u32[]{:S(2)}) copy-start(s32[2,32]{1,0:T(2,128)} %param.11) | copy-start | bytes 772
where the time goes:
time: 429 us; the launch traced here: 428 us
  blocking collectives  379 us (88%)
  other arithmetic  28.4 us (7%)
  local copies, waits for them, and re-layouts  11 us (3%)
  matrix products  9.04 us (2%)
    all_gather x16, blocking collectives, apply_slots(): lax.all_gather(current.astype(jnp.bfloat16), 'row', axis=1, tiled=True)  212 us
    psum x16, blocking collectives, apply_slots(): total = lax.psum(product.astype(jnp.bfloat16), 'col').astype(jnp.float32)  123 us
    psum x2, blocking collectives, orthonormal(): gram = lax.psum(part_gram, 'row') / total_rows  34.8 us
    another operation x6, other arithmetic, orthonormal(): lower = jnp.linalg.cholesky(gram)  13 us
    another operation x4, other arithmetic, orthonormal(): solved = jax.scipy.linalg.solve_triangular(lower, both, lower=True)  11.1 us
    gather x16, local copies, waits for them, and re-layouts, apply_slots(): picked = jnp.take(blocks, local_pattern, axis=1)  9.63 us

commit v1 on v0

--- a/solution.py
+++ b/solution.py
@@ -7,6 +7,12 @@
 ITERS = 2
 HALF_WIDTH = 2.0
 EPSILON = 1e-06
+
+
+def number_the_points(body, ndim_at):
+    row_out = list(body.shape[1:])
+    row_out[ndim_at] *= body.shape[0]
+    return jnp.moveaxis(body, 0, ndim_at).reshape(row_out)
 
 
 def row_scaling(square_sums, live_counts, block):
@@ -51,7 +57,25 @@
     scaling = row_scaling(square_sums, counts, block)
 
     def apply_slots(current):
-        whole = lax.all_gather(current.astype(jnp.bfloat16), "row", axis=1, tiled=True)
+
+        def scenes_point(raw, across, d_out):
+            p_count = lax.axis_size(across)
+            ledger = list(map(lambda dd: (dd, (dd + 1) % p_count), range(p_count)))
+            sides = [(u, no) for no, u in ledger]
+            extra, arr_now = ([], [])
+            for k0 in range(p_count - 1):
+                if k0 % 2 == 0:
+                    extra.append(lax.ppermute(extra[-1] if extra else raw, across, perm=ledger))
+                else:
+                    arr_now.append(
+                        lax.ppermute(arr_now[-1] if arr_now else raw, across, perm=sides)
+                    )
+            reply = jnp.stack([*extra[::-1], raw, *arr_now])
+            everything = lax.axis_index(across) - len(extra)
+            reply = reply[(jnp.arange(p_count) - everything) % p_count]
+            return number_the_points(reply, d_out)
+
+        whole = scenes_point(current.astype(jnp.bfloat16), across="row", d_out=1)
         blocks = whole.reshape(vec_cols, -1, block)
         picked = jnp.take(blocks, local_pattern, axis=1)
         product = jnp.einsum("cbkn,bkmn->cbm", picked, masked, preferred_element_type=jnp.float32)

time: 429 us -> 403 us (0.939)
  blocking collectives: 379 us -> 163 us
  waiting for transfers between devices: 0 us -> 113 us
  starting transfers between devices: 0 us -> 63.5 us
  local copies, waits for them, and re-layouts: 11 us -> 21.4 us
    all_gather x16 -> x0, blocking collectives: 212 us -> none  [apply_slots(): lax.all_gather(current.astype(jnp.bfloat16), 'row', axis=1, tiled=True)]
    ppermute x0 -> x48, waiting for transfers between devices: none -> 113 us  [the longest x32 113 us: scenes_point(): extra.append(lax.ppermute(extra[-1] if extra else raw, across, perm=ledger))]
    ppermute x0 -> x48, starting transfers between devices: none -> 63.5 us  [the longest x16 62.3 us: scenes_point(): lax.ppermute(arr_now[-1] if arr_now else raw, across, perm=sides)]
    gather x0 -> x16, local copies, waits for them, and re-layouts: none -> 8.82 us  [scenes_point(): reply = reply[(jnp.arange(p_count) - everything) % p_count]]
  transfers between devices with their start and end apart: 0 -> 48, of which waited for: 0 -> 31; matrix products, arithmetic and copies ran while one was open for 0% -> 1% of each run, Pallas kernels for 0% -> 0%
where the time goes in v1:
time: 403 us; the launch traced here: 402 us
  blocking collectives  163 us (40%)
  waiting for transfers between devices  113 us (28%)
  starting transfers between devices  63.5 us (16%)
  other arithmetic  30.2 us (7%)
  local copies, waits for them, and re-layouts  21.4 us (5%)
  matrix products  9.03 us (2%)
    psum x16, blocking collectives, apply_slots(): total = lax.psum(product.astype(jnp.bfloat16), 'col').astype(jnp.float32)  123 us
    ppermute x32, waiting for transfers between devices, scenes_point(): extra.append(lax.ppermute(extra[-1] if extra else raw, across, perm=ledger))  113 us
    ppermute x16, starting transfers between devices, scenes_point(): lax.ppermute(arr_now[-1] if arr_now else raw, across, perm=sides)  62.3 us
    psum x2, blocking collectives, orthonormal(): gram = lax.psum(part_gram, 'row') / total_rows  31.5 us
    another operation x6, other arithmetic, orthonormal(): lower = jnp.linalg.cholesky(gram)  13 us
    another operation x4, other arithmetic, orthonormal(): solved = jax.scipy.linalg.solve_triangular(lower, both, lower=True)  11.1 us
    gather x16, local copies, waits for them, and re-layouts, apply_slots(): picked = jnp.take(blocks, local_pattern, axis=1)  9.63 us
    gather x16, local copies, waits for them, and re-layouts, scenes_point(): reply = reply[(jnp.arange(p_count) - everything) % p_count]  8.82 us
  transfers between devices with their start and end apart: 48, of which 31 were waited for; matrix products, arithmetic and copies ran while one was open for 1% of the time, Pallas kernels for 0%

profile of v1, /device:TPU:0, one launch (start us, length us, event | category | flops | bytes accessed | tf_op | source)
XLA Modules:
  0.0 401.8 jit_solution(5434419362011797606)
XLA Ops:
  23.0 8.2 %psum.133 = bf16[32,2,128]{2,0,1:T(8,128)(2,1)S(1)} all-reduce(bf16[32,2,128]{2,0,1:T(8,128)(2,1)S(1)} %fusion.32), channel_id=1, replica_groups=mesh['grp'=2,'row'=4,'col'=2,'vec'=2] {'col'}, use_global_device_ids=true, to_apply=%region_0.2 | all-reduce | flops 8192 | bytes 32768 | tf_op jit(solution)/shard_map/psum | solution.py:82
  44.2 7.2 %psum.135 = bf16[32,256]{1,0:T(8,128)(2,1)S(1)} all-reduce(bf16[32,256]{1,0:T(8,128)(2,1)S(1)} %bitcast.495), channel_id=1, replica_groups=mesh['grp'=2,'row'=4,'col'=2,'vec'=2] {'col'}, use_global_device_ids=true, to_apply=%region_2.4 | all-reduce | flops 8192 | bytes 32768 | tf_op jit(solution)/shard_map/psum | solution.py:82
  57.0 5.5 %collective-permute-done.7 = bf16[32,256]{1,0:T(8,128)(2,1)S(1)} collective-permute-done((bf16[32,256]{1,0:T(8,128)(2,1)S(1)}, bf16[32,256]{1,0:T(8,128)(2,1)S(1)}, u32[]{:S(2)}, u32[]{:S(2)}) %collective-permute-start.7) | collective-permute-done | bytes 16416 | tf_op jit(solution)/shard_map/ppermute | solution.py:68
  64.3 8.2 %psum.136 = bf16[32,2,128]{2,0,1:T(8,128)(2,1)S(1)} all-reduce(bf16[32,2,128]{2,0,1:T(8,128)(2,1)S(1)} %fusion.30), channel_id=1, replica_groups=mesh['grp'=2,'row'=4,'col'=2,'vec'=2] {'col'}, use_global_device_ids=true, to_apply=%region_3.5 | all-reduce | flops 8192 | bytes 32768 | tf_op jit(solution)/shard_map/psum | solution.py:82
  85.5 7.2 %psum.137 = bf16[32,256]{1,0:T(8,128)(2,1)S(1)} all-reduce(bf16[32,256]{1,0:T(8,128)(2,1)S(1)} %bitcast.496), channel_id=1, replica_groups=mesh['grp'=2,'row'=4,'col'=2,'vec'=2] {'col'}, use_global_device_ids=true, to_apply=%region_4.6 | all-reduce | flops 8192 | bytes 32768 | tf_op jit(solution)/shard_map/psum | solution.py:82
  98.3 5.5 %collective-permute-done.13 = bf16[32,256]{1,0:T(8,128)(2,1)S(1)} collective-permute-done((bf16[32,256]{1,0:T(8,128)(2,1)S(1)}, bf16[32,256]{1,0:T(8,128)(2,1)S(1)}, u32[]{:S(2)}, u32[]{:S(2)}) %collective-permute-start.13) | collective-permute-done | bytes 16416 | tf_op jit(solution)/shard_map/ppermute | solution.py:68
  105.6 8.2 %psum.138 = bf16[32,2,128]{2,0,1:T(8,128)(2,1)S(1)} all-reduce(bf16[32,2,128]{2,0,1:T(8,128)(2,1)S(1)} %fusion.28), channel_id=1, replica_groups=mesh['grp'=2,'row'=4,'col'=2,'vec'=2] {'col'}, use_global_device_ids=true, to_apply=%region_5.7 | all-reduce | flops 8192 | bytes 32768 | tf_op jit(solution)/shard_map/psum | solution.py:82
  126.8 7.2 %psum.139 = bf16[32,256]{1,0:T(8,128)(2,1)S(1)} all-reduce(bf16[32,256]{1,0:T(8,128)(2,1)S(1)} %bitcast.497), channel_id=1, replica_groups=mesh['grp'=2,'row'=4,'col'=2,'vec'=2] {'col'}, use_global_device_ids=true, to_apply=%region_6.8 | all-reduce | flops 8192 | bytes 32768 | tf_op jit(solution)/shard_map/psum | solution.py:82
  147.0 8.2 %psum.140 = bf16[32,2,128]{2,0,1:T(8,128)(2,1)S(1)} all-reduce(bf16[32,2,128]{2,0,1:T(8,128)(2,1)S(1)} %fusion.26), channel_id=1, replica_groups=mesh['grp'=2,'row'=4,'col'=2,'vec'=2] {'col'}, use_global_device_ids=true, to_apply=%region_7.9 | all-reduce | flops 8192 | bytes 32768 | tf_op jit(solution)/shard_map/psum | solution.py:82
  168.2 7.2 %psum.141 = bf16[32,256]{1,0:T(8,128)(2,1)S(1)} all-reduce(bf16[32,256]{1,0:T(8,128)(2,1)S(1)} %bitcast.498), channel_id=1, replica_groups=mesh['grp'=2,'row'=4,'col'=2,'vec'=2] {'col'}, use_global_device_ids=true, to_apply=%region_8.10 | all-reduce | flops 8192 | bytes 32768 | tf_op jit(solution)/shard_map/psum | solution.py:82
  177.3 15.8 %psum.142 = f32[64,64]{0,1:T(8,128)S(1)} all-reduce(f32[64,64]{0,1:T(8,128)S(1)} %fusion.158), channel_id=1, replica_groups=mesh['grp'=2,'row'=4,'col'=2,'vec'=2] {'row'}, use_global_device_ids=true, to_apply=%region_9.11 | all-reduce | flops 4096 | bytes 32768 | tf_op jit(solution)/shard_map/psum | solution.py:35
  193.2 5.8 %cholesky.44 = f32[64,64]{1,0:T(8,128)S(1)} custom-call(f32[64,64]{1,0:T(8,128)S(1)} %fusion.120), custom_call_target="Cholesky" | custom-call | tf_op jit(solution)/shard_map/jit(cholesky)/cholesky | solution.py:36
  218.5 8.2 %psum.143 = bf16[32,2,128]{2,0,1:T(8,128)(2,1)S(1)} all-reduce(bf16[32,2,128]{2,0,1:T(8,128)(2,1)S(1)} %fusion.24), channel_id=1, replica_groups=mesh['grp'=2,'row'=4,'col'=2,'vec'=2] {'col'}, use_global_device_ids=true, to_apply=%region_12.16 | all-reduce | flops 8192 | bytes 32768 | tf_op jit(solution)/shard_map/psum | solution.py:82
  239.9 7.2 %psum.144 = bf16[32,256]{1,0:T(8,128)(2,1)S(1)} all-reduce(bf16[32,256]{1,0:T(8,128)(2,1)S(1)} %bitcast.499), channel_id=1, replica_groups=mesh['grp'=2,'row'=4,'col'=2,'vec'=2] {'col'}, use_global_device_ids=true, to_apply=%region_13.17 | all-reduce | flops 8192 | bytes 32768 | tf_op jit(solution)/shard_map/psum | solution.py:82
  252.6 5.5 %collective-permute-done.31 = bf16[32,256]{1,0:T(8,128)(2,1)S(1)} collective-permute-done((bf16[32,256]{1,0:T(8,128)(2,1)S(1)}, bf16[32,256]{1,0:T(8,128)(2,1)S(1)}, u32[]{:S(2)}, u32[]{:S(2)}) %collective-permute-start.31) | collective-permute-done | bytes 16416 | tf_op jit(solution)/shard_map/ppermute | solution.py:68
  260.0 8.3 %psum.145 = bf16[32,2,128]{2,0,1:T(8,128)(2,1)S(1)} all-reduce(bf16[32,2,128]{2,0,1:T(8,128)(2,1)S(1)} %fusion.22), channel_id=1, replica_groups=mesh['grp'=2,'row'=4,'col'=2,'vec'=2] {'col'}, use_global_device_ids=true, to_apply=%region_14.18 | all-reduce | flops 8192 | bytes 32768 | tf_op jit(solution)/shard_map/psum | solution.py:82
  281.3 7.1 %psum.146 = bf16[32,256]{1,0:T(8,128)(2,1)S(1)} all-reduce(bf16[32,256]{1,0:T(8,128)(2,1)S(1)} %bitcast.500), channel_id=1, replica_groups=mesh['grp'=2,'row'=4,'col'=2,'vec'=2] {'col'}, use_global_device_ids=true, to_apply=%region_15.19 | all-reduce | flops 8192 | bytes 32768 | tf_op jit(solution)/shard_map/psum | solution.py:82
  301.3 8.3 %psum.147 = bf16[32,2,128]{2,0,1:T(8,128)(2,1)S(1)} all-reduce(bf16[32,2,128]{2,0,1:T(8,128)(2,1)S(1)} %fusion.20), channel_id=1, replica_groups=mesh['grp'=2,'row'=4,'col'=2,'vec'=2] {'col'}, use_global_device_ids=true, to_apply=%region_16.20 | all-reduce | flops 8192 | bytes 32768 | tf_op jit(solution)/shard_map/psum | solution.py:82
  322.6 7.0 %psum.148 = bf16[32,256]{1,0:T(8,128)(2,1)S(1)} all-reduce(bf16[32,256]{1,0:T(8,128)(2,1)S(1)} %bitcast.501), channel_id=1, replica_groups=mesh['grp'=2,'row'=4,'col'=2,'vec'=2] {'col'}, use_global_device_ids=true, to_apply=%region_17.21 | all-reduce | flops 8192 | bytes 32768 | tf_op jit(solution)/shard_map/psum | solution.py:82
  335.3 5.5 %collective-permute-done.43 = bf16[32,256]{1,0:T(8,128)(2,1)S(1)} collective-permute-done((bf16[32,256]{1,0:T(8,128)(2,1)S(1)}, bf16[32,256]{1,0:T(8,128)(2,1)S(1)}, u32[]{:S(2)}, u32[]{:S(2)}) %collective-permute-start.43) | collective-permute-done | bytes 16416 | tf_op jit(solution)/shard_map/ppermute | solution.py:68
  342.6 8.3 %psum.149 = bf16[32,2,128]{2,0,1:T(8,128)(2,1)S(1)} all-reduce(bf16[32,2,128]{2,0,1:T(8,128)(2,1)S(1)} %fusion.18), channel_id=1, replica_groups=mesh['grp'=2,'row'=4,'col'=2,'vec'=2] {'col'}, use_global_device_ids=true, to_apply=%region_18.22 | all-reduce | flops 8192 | bytes 32768 | tf_op jit(solution)/shard_map/psum | solution.py:82
  363.9 7.0 %psum.150 = bf16[32,256]{1,0:T(8,128)(2,1)S(1)} all-reduce(bf16[32,256]{1,0:T(8,128)(2,1)S(1)} %bitcast.502), channel_id=1, replica_groups=mesh['grp'=2,'row'=4,'col'=2,'vec'=2] {'col'}, use_global_device_ids=true, to_apply=%region_19.23 | all-reduce | flops 8192 | bytes 32768 | tf_op jit(solution)/shard_map/psum | solution.py:82
  373.0 15.8 %psum.151 = f32[64,64]{0,1:T(8,128)S(1)} all-reduce(f32[64,64]{0,1:T(8,128)S(1)} %fusion.159), channel_id=1, replica_groups=mesh['grp'=2,'row'=4,'col'=2,'vec'=2] {'row'}, use_global_device_ids=true, to_apply=%region_20.24 | all-reduce | flops 4096 | bytes 32768 | tf_op jit(solution)/shard_map/psum | solution.py:35
  388.8 5.8 %cholesky.55 = f32[64,64]{1,0:T(8,128)S(1)} custom-call(f32[64,64]{1,0:T(8,128)S(1)} %fusion.118), custom_call_target="Cholesky" | custom-call | tf_op jit(solution)/shard_map/jit(cholesky)/cholesky | solution.py:36
  (295 shorter events, 212.4 us)
Async XLA Ops:
  0.8 14.9 %collective-permute-start.2 = (bf16[32,256]{1,0:T(8,128)(2,1)S(1)}, bf16[32,256]{1,0:T(8,128)(2,1)S(1)}, u32[]{:S(2)}, u32[]{:S(2)}) collective-permute-start(bf16[32,256]{1,0:T(8,128)(2,1)S(1)} %convert_element_type.271), channel_id=1, source_target_pairs={{4,0},{8,4},{12,8},{0,12},{5,1},{9,5},{13,9},{1,13},{6,2},{10,6},{... | collective-permute-start | bytes 49160 | tf_op jit(solution)/shard_map/ppermute | solution.py:71
  5.8 9.8 %collective-permute-start = (bf16[32,256]{1,0:T(8,128)(2,1)S(1)}, bf16[32,256]{1,0:T(8,128)(2,1)S(1)}, u32[]{:S(2)}, u32[]{:S(2)}) collective-permute-start(bf16[32,256]{1,0:T(8,128)(2,1)S(1)} %convert_element_type.271), channel_id=1, source_target_pairs={{0,4},{4,8},{8,12},{12,0},{1,5},{5,9},{9,13},{13,1},{2,6},{6,10},{... | collective-permute-start | bytes 49160 | tf_op jit(solution)/shard_map/ppermute | solution.py:68
  15.6 5.6 %collective-permute-start.1 = (bf16[32,256]{1,0:T(8,128)(2,1)S(1)}, bf16[32,256]{1,0:T(8,128)(2,1)S(1)}, u32[]{:S(2)}, u32[]{:S(2)}) collective-permute-start(bf16[32,256]{1,0:T(8,128)(2,1)S(1)} %collective-permute-done), channel_id=1, source_target_pairs={{0,4},{4,8},{8,12},{12,0},{1,5},{5,9},{9,13},{13,1},{2,6},{6,10},{... | collective-permute-start | bytes 49160 | tf_op jit(solution)/shard_map/ppermute | solution.py:68
  31.2 5.6 %collective-permute-start.3 = (bf16[32,256]{1,0:T(8,128)(2,1)S(1)}, bf16[32,256]{1,0:T(8,128)(2,1)S(1)}, u32[]{:S(2)}, u32[]{:S(2)}) collective-permute-start(bf16[32,256]{1,0:T(8,128)(2,1)S(1)} %fusion.123), channel_id=1, source_target_pairs={{0,4},{4,8},{8,12},{12,0},{1,5},{5,9},{9,13},{13,1},{2,6},{6,10},{... | collective-permute-start | bytes 49160 | tf_op jit(solution)/shard_map/ppermute | solution.py:68
  31.3 5.5 %collective-permute-start.5 = (bf16[32,256]{1,0:T(8,128)(2,1)S(1)}, bf16[32,256]{1,0:T(8,128)(2,1)S(1)}, u32[]{:S(2)}, u32[]{:S(2)}) collective-permute-start(bf16[32,256]{1,0:T(8,128)(2,1)S(1)} %fusion.123), channel_id=1, source_target_pairs={{4,0},{8,4},{12,8},{0,12},{5,1},{9,5},{13,9},{1,13},{6,2},{10,6},{... | collective-permute-start | bytes 49160 | tf_op jit(solution)/shard_map/ppermute | solution.py:71
  51.4 5.6 %collective-permute-start.6 = (bf16[32,256]{1,0:T(8,128)(2,1)S(1)}, bf16[32,256]{1,0:T(8,128)(2,1)S(1)}, u32[]{:S(2)}, u32[]{:S(2)}) collective-permute-start(bf16[32,256]{1,0:T(8,128)(2,1)S(1)} %fusion.125), channel_id=1, source_target_pairs={{0,4},{4,8},{8,12},{12,0},{1,5},{5,9},{9,13},{13,1},{2,6},{6,10},{... | collective-permute-start | bytes 49160 | tf_op jit(solution)/shard_map/ppermute | solution.py:68
  72.5 5.6 %collective-permute-start.9 = (bf16[32,256]{1,0:T(8,128)(2,1)S(1)}, bf16[32,256]{1,0:T(8,128)(2,1)S(1)}, u32[]{:S(2)}, u32[]{:S(2)}) collective-permute-start(bf16[32,256]{1,0:T(8,128)(2,1)S(1)} %fusion.156), channel_id=1, source_target_pairs={{0,4},{4,8},{8,12},{12,0},{1,5},{5,9},{9,13},{13,1},{2,6},{6,10},{... | collective-permute-start | bytes 49160 | tf_op jit(solution)/shard_map/ppermute | solution.py:68
  72.6 5.6 %collective-permute-start.11 = (bf16[32,256]{1,0:T(8,128)(2,1)S(1)}, bf16[32,256]{1,0:T(8,128)(2,1)S(1)}, u32[]{:S(2)}, u32[]{:S(2)}) collective-permute-start(bf16[32,256]{1,0:T(8,128)(2,1)S(1)} %fusion.156), channel_id=1, source_target_pairs={{4,0},{8,4},{12,8},{0,12},{5,1},{9,5},{13,9},{1,13},{6,2},{10,6},{... | collective-permute-start | bytes 49160 | tf_op jit(solution)/shard_map/ppermute | solution.py:71
  92.7 5.6 %collective-permute-start.12 = (bf16[32,256]{1,0:T(8,128)(2,1)S(1)}, bf16[32,256]{1,0:T(8,128)(2,1)S(1)}, u32[]{:S(2)}, u32[]{:S(2)}) collective-permute-start(bf16[32,256]{1,0:T(8,128)(2,1)S(1)} %fusion.155), channel_id=1, source_target_pairs={{0,4},{4,8},{8,12},{12,0},{1,5},{5,9},{9,13},{13,1},{2,6},{6,10},{... | collective-permute-start | bytes 49160 | tf_op jit(solution)/shard_map/ppermute | solution.py:68
  113.9 5.6 %collective-permute-start.15 = (bf16[32,256]{1,0:T(8,128)(2,1)S(1)}, bf16[32,256]{1,0:T(8,128)(2,1)S(1)}, u32[]{:S(2)}, u32[]{:S(2)}) collective-permute-start(bf16[32,256]{1,0:T(8,128)(2,1)S(1)} %fusion.130), channel_id=1, source_target_pairs={{0,4},{4,8},{8,12},{12,0},{1,5},{5,9},{9,13},{13,1},{2,6},{6,10},{... | collective-permute-start | bytes 49160 | tf_op jit(solution)/shard_map/ppermute | solution.py:68
  113.9 5.5 %collective-permute-start.17 = (bf16[32,256]{1,0:T(8,128)(2,1)S(1)}, bf16[32,256]{1,0:T(8,128)(2,1)S(1)}, u32[]{:S(2)}, u32[]{:S(2)}) collective-permute-start(bf16[32,256]{1,0:T(8,128)(2,1)S(1)} %fusion.130), channel_id=1, source_target_pairs={{4,0},{8,4},{12,8},{0,12},{5,1},{9,5},{13,9},{1,13},{6,2},{10,6},{... | collective-permute-start | bytes 49160 | tf_op jit(solution)/shard_map/ppermute | solution.py:71
  134.0 5.6 %collective-permute-start.18 = (bf16[32,256]{1,0:T(8,128)(2,1)S(1)}, bf16[32,256]{1,0:T(8,128)(2,1)S(1)}, u32[]{:S(2)}, u32[]{:S(2)}) collective-permute-start(bf16[32,256]{1,0:T(8,128)(2,1)S(1)} %fusion.126), channel_id=1, source_target_pairs={{0,4},{4,8},{8,12},{12,0},{1,5},{5,9},{9,13},{13,1},{2,6},{6,10},{... | collective-permute-start | bytes 49160 | tf_op jit(solution)/shard_map/ppermute | solution.py:68
  155.2 5.6 %collective-permute-start.21 = (bf16[32,256]{1,0:T(8,128)(2,1)S(1)}, bf16[32,256]{1,0:T(8,128)(2,1)S(1)}, u32[]{:S(2)}, u32[]{:S(2)}) collective-permute-start(bf16[32,256]{1,0:T(8,128)(2,1)S(1)} %fusion.112), channel_id=1, source_target_pairs={{0,4},{4,8},{8,12},{12,0},{1,5},{5,9},{9,13},{13,1},{2,6},{6,10},{... | collective-permute-start | bytes 49160 | tf_op jit(solution)/shard_map/ppermute | solution.py:68
  205.6 5.6 %collective-permute-start.24 = (bf16[32,256]{1,0:T(8,128)(2,1)S(1)}, bf16[32,256]{1,0:T(8,128)(2,1)S(1)}, u32[]{:S(2)}, u32[]{:S(2)}) collective-permute-start(bf16[32,256]{1,0:T(8,128)(2,1)S(1)} %dynamic-slice_convert_fusion), channel_id=1, source_target_pairs={{0,4},{4,8},{8,12},{12,0},{1,5},{5,9},{9,13},{13,1},{2,6},{6,10},{... | collective-permute-start | bytes 49160 | tf_op jit(solution)/shard_map/ppermute | solution.py:68
  226.7 5.8 %collective-permute-start.27 = (bf16[32,256]{1,0:T(8,128)(2,1)S(1)}, bf16[32,256]{1,0:T(8,128)(2,1)S(1)}, u32[]{:S(2)}, u32[]{:S(2)}) collective-permute-start(bf16[32,256]{1,0:T(8,128)(2,1)S(1)} %fusion.124), channel_id=1, source_target_pairs={{0,4},{4,8},{8,12},{12,0},{1,5},{5,9},{9,13},{13,1},{2,6},{6,10},{... | collective-permute-start | bytes 49160 | tf_op jit(solution)/shard_map/ppermute | solution.py:68
  227.0 5.5 %collective-permute-start.29 = (bf16[32,256]{1,0:T(8,128)(2,1)S(1)}, bf16[32,256]{1,0:T(8,128)(2,1)S(1)}, u32[]{:S(2)}, u32[]{:S(2)}) collective-permute-start(bf16[32,256]{1,0:T(8,128)(2,1)S(1)} %fusion.124), channel_id=1, source_target_pairs={{4,0},{8,4},{12,8},{0,12},{5,1},{9,5},{13,9},{1,13},{6,2},{10,6},{... | collective-permute-start | bytes 49160 | tf_op jit(solution)/shard_map/ppermute | solution.py:71
  247.0 5.6 %collective-permute-start.30 = (bf16[32,256]{1,0:T(8,128)(2,1)S(1)}, bf16[32,256]{1,0:T(8,128)(2,1)S(1)}, u32[]{:S(2)}, u32[]{:S(2)}) collective-permute-start(bf16[32,256]{1,0:T(8,128)(2,1)S(1)} %fusion.154), channel_id=1, source_target_pairs={{0,4},{4,8},{8,12},{12,0},{1,5},{5,9},{9,13},{13,1},{2,6},{6,10},{... | collective-permute-start | bytes 49160 | tf_op jit(solution)/shard_map/ppermute | solution.py:68
  268.3 5.6 %collective-permute-start.33 = (bf16[32,256]{1,0:T(8,128)(2,1)S(1)}, bf16[32,256]{1,0:T(8,128)(2,1)S(1)}, u32[]{:S(2)}, u32[]{:S(2)}) collective-permute-start(bf16[32,256]{1,0:T(8,128)(2,1)S(1)} %fusion.157), channel_id=1, source_target_pairs={{0,4},{4,8},{8,12},{12,0},{1,5},{5,9},{9,13},{13,1},{2,6},{6,10},{... | collective-permute-start | bytes 49160 | tf_op jit(solution)/shard_map/ppermute | solution.py:68
  268.4 5.5 %collective-permute-start.35 = (bf16[32,256]{1,0:T(8,128)(2,1)S(1)}, bf16[32,256]{1,0:T(8,128)(2,1)S(1)}, u32[]{:S(2)}, u32[]{:S(2)}) collective-permute-start(bf16[32,256]{1,0:T(8,128)(2,1)S(1)} %fusion.157), channel_id=1, source_target_pairs={{4,0},{8,4},{12,8},{0,12},{5,1},{9,5},{13,9},{1,13},{6,2},{10,6},{... | collective-permute-start | bytes 49160 | tf_op jit(solution)/shard_map/ppermute | solution.py:71
  288.4 5.6 %collective-permute-start.36 = (bf16[32,256]{1,0:T(8,128)(2,1)S(1)}, bf16[32,256]{1,0:T(8,128)(2,1)S(1)}, u32[]{:S(2)}, u32[]{:S(2)}) collective-permute-start(bf16[32,256]{1,0:T(8,128)(2,1)S(1)} %fusion.127), channel_id=1, source_target_pairs={{0,4},{4,8},{8,12},{12,0},{1,5},{5,9},{9,13},{13,1},{2,6},{6,10},{... | collective-permute-start | bytes 49160 | tf_op jit(solution)/shard_map/ppermute | solution.py:68
  309.6 5.6 %collective-permute-start.39 = (bf16[32,256]{1,0:T(8,128)(2,1)S(1)}, bf16[32,256]{1,0:T(8,128)(2,1)S(1)}, u32[]{:S(2)}, u32[]{:S(2)}) collective-permute-start(bf16[32,256]{1,0:T(8,128)(2,1)S(1)} %fusion.131), channel_id=1, source_target_pairs={{0,4},{4,8},{8,12},{12,0},{1,5},{5,9},{9,13},{13,1},{2,6},{6,10},{... | collective-permute-start | bytes 49160 | tf_op jit(solution)/shard_map/ppermute | solution.py:68
  309.7 5.5 %collective-permute-start.41 = (bf16[32,256]{1,0:T(8,128)(2,1)S(1)}, bf16[32,256]{1,0:T(8,128)(2,1)S(1)}, u32[]{:S(2)}, u32[]{:S(2)}) collective-permute-start(bf16[32,256]{1,0:T(8,128)(2,1)S(1)} %fusion.131), channel_id=1, source_target_pairs={{4,0},{8,4},{12,8},{0,12},{5,1},{9,5},{13,9},{1,13},{6,2},{10,6},{... | collective-permute-start | bytes 49160 | tf_op jit(solution)/shard_map/ppermute | solution.py:71
  329.7 5.6 %collective-permute-start.42 = (bf16[32,256]{1,0:T(8,128)(2,1)S(1)}, bf16[32,256]{1,0:T(8,128)(2,1)S(1)}, u32[]{:S(2)}, u32[]{:S(2)}) collective-permute-start(bf16[32,256]{1,0:T(8,128)(2,1)S(1)} %fusion.132), channel_id=1, source_target_pairs={{0,4},{4,8},{8,12},{12,0},{1,5},{5,9},{9,13},{13,1},{2,6},{6,10},{... | collective-permute-start | bytes 49160 | tf_op jit(solution)/shard_map/ppermute | solution.py:68
  351.0 5.6 %collective-permute-start.45 = (bf16[32,256]{1,0:T(8,128)(2,1)S(1)}, bf16[32,256]{1,0:T(8,128)(2,1)S(1)}, u32[]{:S(2)}, u32[]{:S(2)}) collective-permute-start(bf16[32,256]{1,0:T(8,128)(2,1)S(1)} %fusion.105), channel_id=1, source_target_pairs={{0,4},{4,8},{8,12},{12,0},{1,5},{5,9},{9,13},{13,1},{2,6},{6,10},{... | collective-permute-start | bytes 49160 | tf_op jit(solution)/shard_map/ppermute | solution.py:68
  (27 other events, 169.7 us)
